TPU v7x, 512 devices: a whole 4x8x8 slice. The times are simulated.
512 devices in a mesh: freq: 16 (over y, core), trace: 32 (over z, x).
Axes of the slice: x: 4, y: 8, z: 8, core: 2. Of those that a mesh axis runs over, the one named last changes fastest.
Arguments:
- traces: bfloat16 [64, 128, 2048], P('trace', 'freq'), may hold values from -20 to 20
- omega: float32 [2, 33, 64, 64], replicated, may hold values from -0.125 to 0.125
Outputs:
- denoised: float32 [64, 128, 2048], P('trace', 'freq')
All inputs are finite; a program needn't handle non-finite values.
Results may differ from a plain program's by a relative error of at most 0.0003.
Values sent between devices are 32-bit elements; how exact they have to be, the bound alone decides.
No kernel may reach another device: no remote copies, remote signals or barrier semaphores. Data moves between devices by JAX's collectives and lax.ppermute only.
A program may use at most 64 MiB of HBM per device.

v0:
```python
import math
import jax
import jax.numpy as jnp
from jax import lax
from jax.sharding import PartitionSpec as P

FREQ_DEV = 1
highest = lax.Precision.HIGHEST


def fourier_tables(samples, freq_total):
    moments = jnp.arange(samples, dtype=jnp.int32)
    bins = jnp.arange(freq_total, dtype=jnp.int32) + 1
    phases = bins[:, None] * moments[None, :] % samples
    angles = phases.astype(jnp.float32) * (2.0 * math.pi / samples)
    return (jnp.cos(angles), jnp.sin(angles))


def anti_counts(spots, length, window, lags):
    counted = jnp.minimum(jnp.minimum(spots + 1, length - spots), min(window, lags))
    return counted.astype(jnp.float32)


def solve_one(factor, right_side):
    return jax.scipy.linalg.cho_solve((factor, True), right_side)


def body(traces, omega):
    rows_dev, cols_dev, samples = traces.shape
    lag_x, lag_y, rank_size = (omega.shape[1], omega.shape[2], omega.shape[3])
    trace_count = lax.axis_size("trace")
    freq_count = lax.axis_size("freq")
    patch_x = rows_dev * trace_count
    patch_y = cols_dev * freq_count
    win_x = patch_x - lag_x + 1
    win_y = patch_y - lag_y + 1
    freq_total = FREQ_DEV * freq_count
    own_rows = win_x // trace_count
    own_lags = lag_y // trace_count
    position = lax.axis_index("trace")
    cosine_table, sine_table = fourier_tables(samples, freq_total)
    norm_scale = 1.0 / math.sqrt(samples)
    forward = jnp.stack([cosine_table.T, -sine_table.T], axis=1) * norm_scale
    spectrum = jnp.einsum("xyt,tpk->xypk", traces.astype(jnp.float32), forward, precision=highest)
    spectrum = lax.all_to_all(spectrum, "freq", split_axis=3, concat_axis=1, tiled=True)
    slices = jnp.transpose(spectrum, (3, 2, 0, 1))
    whole_slices = lax.all_gather(slices, "trace", axis=2, tiled=True)
    freq_dev = whole_slices.shape[0]
    first_row = position * own_rows
    row_slabs = jnp.stack([lax.dynamic_slice_in_dim(whole_slices, first_row + 0, lag_x, 2)], axis=1)
    hankel = jnp.stack([row_slabs[..., anchor : anchor + lag_y] for anchor in range(win_y)], axis=3)
    hankel_flat = hankel.reshape(freq_dev, own_rows * 2 * win_y, lag_x * lag_y)
    omega_flat = omega.reshape(2, lag_x * lag_y, rank_size)
    products = jnp.einsum("fnm,smq->fnsq", hankel_flat, omega_flat, precision=highest)
    products = products.reshape(freq_dev, own_rows, 2, win_y, 2, rank_size)
    sketch_re = products[:, :, 0, :, 0] - products[:, :, 1, :, 1]
    sketch_im = products[:, :, 0, :, 1] + products[:, :, 1, :, 0]
    own_sketch = jnp.transpose(jnp.concatenate([sketch_re, sketch_im], -1), (1, 0, 2, 3))
    sketch = lax.all_gather(own_sketch, "trace", axis=0, tiled=True)
    inner = lax.psum(
        jnp.einsum("afbp,afbq->fpq", own_sketch, own_sketch, precision=highest), "trace"
    )
    lag_start = position * own_lags
    hankel_blocks = []
    for offset in range(own_lags):
        band = lax.dynamic_slice_in_dim(whole_slices, lag_start + offset, win_y, 3)
        hankel_blocks.append(
            jnp.stack([band[:, :, anchor : anchor + win_x] for anchor in range(lag_x)], axis=2)
        )
    columns = jnp.stack(hankel_blocks, axis=1).reshape(
        freq_dev, own_lags * 2 * lag_x, win_x * win_y
    )
    flat_sketch = jnp.transpose(sketch, (1, 0, 2, 3)).reshape(
        freq_dev, win_x * win_y, 2 * rank_size
    )
    project = jnp.einsum("fnm,fmq->fnq", columns, flat_sketch, precision=highest).reshape(
        freq_dev, own_lags, 2, lag_x, 2 * rank_size
    )
    proj_re = jnp.transpose(
        project[:, :, 0, :, :rank_size] + project[:, :, 1, :, rank_size:], (0, 3, 1, 2)
    )
    proj_im = jnp.transpose(
        project[:, :, 1, :, :rank_size] - project[:, :, 0, :, rank_size:], (0, 3, 1, 2)
    )
    gram_re = inner[:, :rank_size, :rank_size] + inner[:, rank_size:, rank_size:]
    gram_im = inner[:, :rank_size, rank_size:] - inner[:, rank_size:, :rank_size]
    real_gram = jnp.concatenate(
        [jnp.concatenate([gram_re, -gram_im], 2), jnp.concatenate([gram_im, gram_re], 2)], 1
    )
    right_side = jnp.concatenate([proj_re, proj_im], 1).reshape(
        freq_dev, 2 * rank_size, own_lags * lag_x
    )
    factor = jnp.linalg.cholesky(real_gram)
    solved = jax.vmap(solve_one)(factor, right_side)
    mix_re = solved[:, :rank_size]
    mix_im = solved[:, rank_size:]
    mix_real = jnp.concatenate([mix_re, -mix_im], 1).reshape(
        freq_dev, 2 * rank_size, own_lags, lag_x
    )
    mix_imag = jnp.concatenate([mix_im, mix_re], 1).reshape(
        freq_dev, 2 * rank_size, own_lags, lag_x
    )
    mixing = jnp.stack([mix_real, mix_imag], axis=3)
    sketch_cols = jnp.transpose(sketch, (1, 2, 3, 0))
    lowrank = jnp.einsum("fqezc,fbqa->fbezca", mixing, sketch_cols, precision=highest)
    target = (
        jnp.arange(lag_x, dtype=jnp.int32)[:, None] + jnp.arange(win_x, dtype=jnp.int32)[None, :]
    ).reshape(-1)
    diagonal = (target[:, None] == jnp.arange(patch_x, dtype=jnp.int32)[None, :]).astype(
        jnp.float32
    )
    spread = jnp.dot(lowrank.reshape(-1, lag_x * win_x), diagonal, precision=highest).reshape(
        freq_dev, win_y, own_lags, 2, patch_x
    )
    partial_value = jnp.zeros((patch_x, freq_dev, 2, patch_y), jnp.float32)
    zero_index = jnp.zeros((), jnp.int32)
    for offset in range(own_lags):
        band_block = jnp.transpose(spread[:, :, offset], (3, 0, 2, 1))
        partial_value = partial_value + lax.dynamic_update_slice(
            jnp.zeros_like(partial_value),
            band_block,
            (zero_index, zero_index, zero_index, lag_start + offset),
        )
    averaged = lax.psum_scatter(partial_value, "trace", scatter_dimension=0, tiled=True)
    spots_x = position * rows_dev + jnp.arange(rows_dev, dtype=jnp.int32)
    spots_y = jnp.arange(patch_y, dtype=jnp.int32)
    counts = (
        anti_counts(spots_x, patch_x, win_x, lag_x)[:, None, None, None]
        * anti_counts(spots_y, patch_y, win_y, lag_y)[None, None, None, :]
    )
    averaged = averaged / counts
    returned = lax.all_to_all(averaged, "freq", split_axis=3, concat_axis=1, tiled=True)
    inverse = jnp.stack([cosine_table, -sine_table], axis=1) * (2.0 * norm_scale)
    return jnp.einsum("xkpy,kpt->xyt", returned, inverse, precision=highest)


def solution(mesh):
    return jax.shard_map(
        body,
        mesh=mesh,
        in_specs=(P("trace", "freq", None), P()),
        out_specs=P("trace", "freq", None),
        check_vma=False,
    )
```

profile of v0, /device:TPU:1, one launch (start us, length us, event | category | flops | bytes accessed | tf_op | source)
XLA Modules:
  0.0 583.4 jit_solution(9340026111584924302)
XLA Ops:
  7.2 1.4 convolution_bitcast_fusion.5
  9.3 10.1 %all-to-all-start = ((f32[2,8,2,16]{1,0,2,3:T(2,128)}), f32[2,8,2,16]{1,0,2,3:T(2,128)S(1)}, u32[]{:S(2)}, u32[]{:S(2)}) async-start(f32[2,8,2,16]{1,0,2,3:T(2,128)} %copy.367), calls=%async_computation | async-start | bytes 65536 | tf_op jit(solution)/shard_map/all_to_all | solution.py:45
  19.5 7.4 %all-to-all-done = f32[2,8,2,16]{1,0,2,3:T(2,128)S(1)} async-done(((f32[2,8,2,16]{1,0,2,3:T(2,128)}), f32[2,8,2,16]{1,0,2,3:T(2,128)S(1)}, u32[]{:S(2)}, u32[]{:S(2)}) %all-to-all-start) | async-done | bytes 2080 | tf_op jit(solution)/shard_map/all_to_all | solution.py:45
  27.0 41.2 %all_gather.6 = f32[1,2,64,128]{3,1,0,2:T(2,128)S(1)} all-gather(f32[1,2,2,128]{3,1,0,2:T(2,128)S(1)} %bitcast.277), channel_id=1, replica_groups=mesh['freq'=16,'trace'=32] {'trace'}, dimensions={2}, use_global_device_ids=true | all-gather | bytes 67584 | tf_op jit(solution)/shard_map/all_gather | solution.py:47
  68.2 1.6 fusion.69
  69.8 1.4 fusion.68
  71.9 1.0 fusion.70
  73.0 0.8 copy.379
  74.4 0.8 copy.380
  75.9 0.8 copy.381
  77.3 0.8 copy.382
  78.8 0.8 copy.383
  80.2 0.8 copy.384
  81.7 0.8 copy.385
  83.1 0.8 copy.386
  84.6 0.8 copy.387
  86.0 0.8 copy.388
  87.5 0.8 copy.389
  88.9 0.8 copy.390
  90.4 0.8 copy.391
  91.8 0.8 copy.392
  93.3 0.8 copy.393
  94.7 0.8 copy.394
  96.2 0.8 copy.395
  97.6 0.8 copy.396
  99.1 0.8 copy.397
  133.9 9.0 %stack.490 = f32[2,65,2112]{2,1,0:T(8,128)S(1)} concatenate(f32[2,1,2112]{2,1,0:T(1,128)} %stack.562, f32[2,1,2112]{2,1,0:T(1,128)} %stack.563, f32[2,1,2112]{2,1,0:T(1,128)} %stack.564, f32[2,1,2112]{2,1,0:T(1,128)} %stack.565, f32[2,1,2112]{2,1,0:T(1,128)} %stack.566, f32[2,1,2112]{2,1,0:T(1,128)} %stack.567, f32[2,1,2112]{2,1,0:T(1,128)} %stack.568, f32[2,1,2112]{2,1,0:T(1,128)} %stack.569, ...), dimensions={1} | concatenate | bytes 2196480 | tf_op jit(solution)/shard_map/stack | solution.py:51
  142.9 3.6 fusion.6
  146.6 0.9 convolution_bitcast_fusion.3
  149.8 1.2 constant_dynamic-slice_fusion.65
  163.3 1.8 constant_dynamic-slice_fusion.47
  199.0 5.5 stack.524
  204.6 6.3 %stack.558 = f32[1,2,33,2080]{3,2,1,0:T(8,128)} concatenate(f32[1,2,1,2080]{3,2,1,0:T(1,128)S(1)} %copy-done.37, f32[1,2,1,2080]{3,2,1,0:T(1,128)} %stack.526, f32[1,2,1,2080]{3,2,1,0:T(1,128)} %stack.527, f32[1,2,1,2080]{3,2,1,0:T(1,128)} %stack.528, f32[1,2,1,2080]{3,2,1,0:T(1,128)S(1)} %copy-done.48, f32[1,2,1,2080]{3,2,1,0:T(1,128)S(1)} %copy-done.49, ...), dimensions={2} | concatenate | bytes 1098240 | tf_op jit(solution)/shard_map/stack | solution.py:68
  211.0 89.0 %all-reduce.4.cloned.1.call-done = f32[1,128,128]{1,2,0:T(8,128)} async-done(((f32[1,128,128]{1,2,0:T(8,128)}), f32[1,128,128]{1,2,0:T(8,128)}) %all-reduce.4.cloned.1.call-update) | async-done | bytes 65552 | tf_op jit(solution)/shard_map/psum | solution.py:60
  299.9 0.9 fusion.66
  301.2 11.9 %custom-call.11 = f32[1,128,128]{2,1,0:T(8,128)S(1)} custom-call(f32[1,128,128]{2,1,0:T(8,128)S(1)} %fusion.46), custom_call_target="Cholesky" | custom-call | tf_op jit(solution)/shard_map/jit(cholesky)/cholesky | solution.py:93
  314.4 9.8 %custom-call.12 = f32[1,1,128,128]{2,3,1,0:T(8,128)S(1)} custom-call(f32[1,1,128,128]{3,2,1,0:T(8,128)S(1)} %fusion.41), custom_call_target="InvertDiagBlocksLowerTriangular" | custom-call | tf_op jit(solution)/shard_map/vmap(jit(_cho_solve))/triangular_solve | solution.py:25
  324.2 58.3 %all-gather.2.cloned.1.call-done = f32[32,1,65,128]{3,1,2,0:T(1,128)} async-done(((f32[1,1,65,128]{3,1,2,0:T(1,128)}), f32[32,1,65,128]{3,1,2,0:T(1,128)}) %all-gather.2.cloned.1.call-update) | async-done | bytes 1064976 | tf_op jit(solution)/shard_map/all_gather | solution.py:59
  382.6 3.1 fusion.9
  386.6 5.1 convolution_bitcast_fusion.1
  391.8 6.0 %copy.575 = f32[1,65,2,2,33,32]{1,5,4,3,2,0:T(8,128)} copy(f32[1,65,2,2,33,32]{4,5,3,2,1,0:T(8,128)} %convolution_bitcast_fusion.1) | data formatting | bytes 2196480 | tf_op jit(solution)/shard_map/fqezc,fbqa->fbezca/transpose | solution.py:105
  397.8 2.6 convolution_bitcast_fusion.2
  402.2 1.3 dynamic-slice.1
  404.1 149.5 %all-reduce.6.cloned.1.call-done = f32[64,1,2,128]{3,0,2,1:T(8,128)} async-done(((f32[64,1,2,128]{3,0,2,1:T(8,128)}), f32[64,1,2,128]{3,0,2,1:T(8,128)}) %all-reduce.6.cloned.1.call-update) | async-done | bytes 65552
  554.3 0.8 copy.577
  555.1 11.8 %all-to-all-start.1 = ((f32[2,1,2,128]{0,2,1,3:T(2,128)}), f32[2,1,2,128]{0,2,1,3:T(2,128)S(1)}, u32[]{:S(2)}, u32[]{:S(2)}) async-start(f32[2,1,2,128]{0,2,1,3:T(2,128)} %copy.577), calls=%async_computation.1 | async-start | bytes 262144 | tf_op jit(solution)/shard_map/all_to_all | solution.py:132
  567.4 8.3 %all-to-all-done.1 = f32[2,1,2,128]{0,2,1,3:T(2,128)S(1)} async-done(((f32[2,1,2,128]{0,2,1,3:T(2,128)}), f32[2,1,2,128]{0,2,1,3:T(2,128)S(1)}, u32[]{:S(2)}, u32[]{:S(2)}) %all-to-all-start.1) | async-done | bytes 2080 | tf_op jit(solution)/shard_map/all_to_all | solution.py:132
  575.9 1.0 convolution_bitcast_fusion
  (402 shorter events, 102.1 us)
Async XLA Ops:
  6.5 136.4 %copy-start = (f32[2,33,64,64]{3,2,1,0:T(8,128)S(1)}, f32[2,33,64,64]{3,2,1,0:T(8,128)}, u32[]{:S(2)}) copy-start(f32[2,33,64,64]{3,2,1,0:T(8,128)} %param.3) | copy-start | bytes 3244036
  9.3 17.6 %all-to-all-start = ((f32[2,8,2,16]{1,0,2,3:T(2,128)}), f32[2,8,2,16]{1,0,2,3:T(2,128)S(1)}, u32[]{:S(2)}, u32[]{:S(2)}) async-start(f32[2,8,2,16]{1,0,2,3:T(2,128)} %copy.367), calls=%async_computation | async-start | bytes 65536 | tf_op jit(solution)/shard_map/all_to_all | solution.py:45
  19.4 280.5 %all-reduce.4.cloned.1.call-start = ((), (), s32[]{:S(2)}) async-start(), calls=%async_computation.3 | async-start | bytes 131072 | tf_op jit(solution)/shard_map/psum | solution.py:60
  113.8 14.5 %copy-start.10 = (f32[1,1,2,33,64]{4,2,3,1,0:T(2,128)S(1)}, f32[1,1,2,33,64]{4,2,3,1,0:T(2,128)}, u32[]{:S(2)}) copy-start(f32[1,1,2,33,64]{4,2,3,1,0:T(2,128)} %get-tuple-element.145) | copy-start | bytes 50692
  114.5 14.5 %copy-start.9 = (f32[1,1,2,33,64]{4,2,3,1,0:T(2,128)S(1)}, f32[1,1,2,33,64]{4,2,3,1,0:T(2,128)}, u32[]{:S(2)}) copy-start(f32[1,1,2,33,64]{4,2,3,1,0:T(2,128)} %get-tuple-element.144) | copy-start | bytes 50692
  115.2 14.6 %copy-start.8 = (f32[1,1,2,33,64]{4,2,3,1,0:T(2,128)S(1)}, f32[1,1,2,33,64]{4,2,3,1,0:T(2,128)}, u32[]{:S(2)}) copy-start(f32[1,1,2,33,64]{4,2,3,1,0:T(2,128)} %get-tuple-element.143) | copy-start | bytes 50692
  115.9 14.5 %copy-start.7 = (f32[1,1,2,33,64]{4,2,3,1,0:T(2,128)S(1)}, f32[1,1,2,33,64]{4,2,3,1,0:T(2,128)}, u32[]{:S(2)}) copy-start(f32[1,1,2,33,64]{4,2,3,1,0:T(2,128)} %get-tuple-element.142) | copy-start | bytes 50692
  116.6 14.5 %copy-start.6 = (f32[1,1,2,33,64]{4,2,3,1,0:T(2,128)S(1)}, f32[1,1,2,33,64]{4,2,3,1,0:T(2,128)}, u32[]{:S(2)}) copy-start(f32[1,1,2,33,64]{4,2,3,1,0:T(2,128)} %get-tuple-element.141) | copy-start | bytes 50692
  117.3 14.5 %copy-start.5 = (f32[1,1,2,33,64]{4,2,3,1,0:T(2,128)S(1)}, f32[1,1,2,33,64]{4,2,3,1,0:T(2,128)}, u32[]{:S(2)}) copy-start(f32[1,1,2,33,64]{4,2,3,1,0:T(2,128)} %get-tuple-element.140) | copy-start | bytes 50692
  118.0 14.6 %copy-start.4 = (f32[1,1,2,33,64]{4,2,3,1,0:T(2,128)S(1)}, f32[1,1,2,33,64]{4,2,3,1,0:T(2,128)}, u32[]{:S(2)}) copy-start(f32[1,1,2,33,64]{4,2,3,1,0:T(2,128)} %get-tuple-element.139) | copy-start | bytes 50692
  118.7 14.5 %copy-start.3 = (f32[1,1,2,33,64]{4,2,3,1,0:T(2,128)S(1)}, f32[1,1,2,33,64]{4,2,3,1,0:T(2,128)}, u32[]{:S(2)}) copy-start(f32[1,1,2,33,64]{4,2,3,1,0:T(2,128)} %get-tuple-element.138) | copy-start | bytes 50692
  119.4 14.6 %copy-start.51 = (f32[2,1,2112]{2,1,0:T(1,128)S(1)}, f32[2,1,2112]{2,1,0:T(1,128)}, u32[]{:S(2)}) copy-start(f32[2,1,2112]{2,1,0:T(1,128)} %stack.571) | copy-start | bytes 50692
  119.4 14.6 %copy-start.52 = (f32[2,1,2112]{2,1,0:T(1,128)S(1)}, f32[2,1,2112]{2,1,0:T(1,128)}, u32[]{:S(2)}) copy-start(f32[2,1,2112]{2,1,0:T(1,128)} %stack.572) | copy-start | bytes 50692
  147.5 235.1 %all-gather.2.cloned.1.call-start = ((), (), s32[]{:S(2)}) async-start(), calls=%async_computation.2 | async-start | bytes 1098240 | tf_op jit(solution)/shard_map/all_gather | solution.py:59
  148.3 405.3 %all-reduce.6.cloned.1.call-start = ((), (), s32[]{:S(2)}) async-start(), calls=%async_computation.4 | async-start | bytes 131072
  188.1 10.6 %copy-start.11 = (f32[1,2,1,2080]{3,2,1,0:T(1,128)S(1)}, f32[1,2,1,2080]{3,2,1,0:T(1,128)}, u32[]{:S(2)}) copy-start(f32[1,2,1,2080]{3,2,1,0:T(1,128)} %stack.491) | copy-start | bytes 49924
  188.1 10.6 %copy-start.12 = (f32[1,2,1,2080]{3,2,1,0:T(1,128)S(1)}, f32[1,2,1,2080]{3,2,1,0:T(1,128)}, u32[]{:S(2)}) copy-start(f32[1,2,1,2080]{3,2,1,0:T(1,128)} %stack.508) | copy-start | bytes 49924
  188.1 10.6 %copy-start.13 = (f32[1,2,1,2080]{3,2,1,0:T(1,128)S(1)}, f32[1,2,1,2080]{3,2,1,0:T(1,128)}, u32[]{:S(2)}) copy-start(f32[1,2,1,2080]{3,2,1,0:T(1,128)} %stack.509) | copy-start | bytes 49924
  188.1 10.6 %copy-start.14 = (f32[1,2,1,2080]{3,2,1,0:T(1,128)S(1)}, f32[1,2,1,2080]{3,2,1,0:T(1,128)}, u32[]{:S(2)}) copy-start(f32[1,2,1,2080]{3,2,1,0:T(1,128)} %stack.510) | copy-start | bytes 49924
  188.2 10.6 %copy-start.15 = (f32[1,2,1,2080]{3,2,1,0:T(1,128)S(1)}, f32[1,2,1,2080]{3,2,1,0:T(1,128)}, u32[]{:S(2)}) copy-start(f32[1,2,1,2080]{3,2,1,0:T(1,128)} %stack.511) | copy-start | bytes 49924
  188.2 10.6 %copy-start.16 = (f32[1,2,1,2080]{3,2,1,0:T(1,128)S(1)}, f32[1,2,1,2080]{3,2,1,0:T(1,128)}, u32[]{:S(2)}) copy-start(f32[1,2,1,2080]{3,2,1,0:T(1,128)} %stack.512) | copy-start | bytes 49924
  188.2 10.6 %copy-start.17 = (f32[1,2,1,2080]{3,2,1,0:T(1,128)S(1)}, f32[1,2,1,2080]{3,2,1,0:T(1,128)}, u32[]{:S(2)}) copy-start(f32[1,2,1,2080]{3,2,1,0:T(1,128)} %stack.513) | copy-start | bytes 49924
  188.2 10.6 %copy-start.18 = (f32[1,2,1,2080]{3,2,1,0:T(1,128)S(1)}, f32[1,2,1,2080]{3,2,1,0:T(1,128)}, u32[]{:S(2)}) copy-start(f32[1,2,1,2080]{3,2,1,0:T(1,128)} %stack.514) | copy-start | bytes 49924
  188.2 10.6 %copy-start.19 = (f32[1,2,1,2080]{3,2,1,0:T(1,128)S(1)}, f32[1,2,1,2080]{3,2,1,0:T(1,128)}, u32[]{:S(2)}) copy-start(f32[1,2,1,2080]{3,2,1,0:T(1,128)} %stack.515) | copy-start | bytes 49924
  188.2 10.6 %copy-start.20 = (f32[1,2,1,2080]{3,2,1,0:T(1,128)S(1)}, f32[1,2,1,2080]{3,2,1,0:T(1,128)}, u32[]{:S(2)}) copy-start(f32[1,2,1,2080]{3,2,1,0:T(1,128)} %stack.516) | copy-start | bytes 49924
  188.2 10.6 %copy-start.21 = (f32[1,2,1,2080]{3,2,1,0:T(1,128)S(1)}, f32[1,2,1,2080]{3,2,1,0:T(1,128)}, u32[]{:S(2)}) copy-start(f32[1,2,1,2080]{3,2,1,0:T(1,128)} %stack.517) | copy-start | bytes 49924
  188.2 10.6 %copy-start.22 = (f32[1,2,1,2080]{3,2,1,0:T(1,128)S(1)}, f32[1,2,1,2080]{3,2,1,0:T(1,128)}, u32[]{:S(2)}) copy-start(f32[1,2,1,2080]{3,2,1,0:T(1,128)} %stack.518) | copy-start | bytes 49924
  188.2 10.6 %copy-start.23 = (f32[1,2,1,2080]{3,2,1,0:T(1,128)S(1)}, f32[1,2,1,2080]{3,2,1,0:T(1,128)}, u32[]{:S(2)}) copy-start(f32[1,2,1,2080]{3,2,1,0:T(1,128)} %stack.519) | copy-start | bytes 49924
  188.2 10.6 %copy-start.24 = (f32[1,2,1,2080]{3,2,1,0:T(1,128)S(1)}, f32[1,2,1,2080]{3,2,1,0:T(1,128)}, u32[]{:S(2)}) copy-start(f32[1,2,1,2080]{3,2,1,0:T(1,128)} %stack.520) | copy-start | bytes 49924
  188.3 10.6 %copy-start.25 = (f32[1,2,1,2080]{3,2,1,0:T(1,128)S(1)}, f32[1,2,1,2080]{3,2,1,0:T(1,128)}, u32[]{:S(2)}) copy-start(f32[1,2,1,2080]{3,2,1,0:T(1,128)} %stack.521) | copy-start | bytes 49924
  188.3 10.6 %copy-start.26 = (f32[1,2,1,2080]{3,2,1,0:T(1,128)S(1)}, f32[1,2,1,2080]{3,2,1,0:T(1,128)}, u32[]{:S(2)}) copy-start(f32[1,2,1,2080]{3,2,1,0:T(1,128)} %stack.522) | copy-start | bytes 49924
  188.3 10.6 %copy-start.27 = (f32[1,2,1,2080]{3,2,1,0:T(1,128)S(1)}, f32[1,2,1,2080]{3,2,1,0:T(1,128)}, u32[]{:S(2)}) copy-start(f32[1,2,1,2080]{3,2,1,0:T(1,128)} %stack.523) | copy-start | bytes 49924
  188.3 10.6 %copy-start.28 = (f32[1,2,1,2080]{3,2,1,0:T(1,128)S(1)}, f32[1,2,1,2080]{3,2,1,0:T(1,128)}, u32[]{:S(2)}) copy-start(f32[1,2,1,2080]{3,2,1,0:T(1,128)} %stack.492) | copy-start | bytes 49924
  188.3 10.6 %copy-start.29 = (f32[1,2,1,2080]{3,2,1,0:T(1,128)S(1)}, f32[1,2,1,2080]{3,2,1,0:T(1,128)}, u32[]{:S(2)}) copy-start(f32[1,2,1,2080]{3,2,1,0:T(1,128)} %stack.493) | copy-start | bytes 49924
  188.3 10.6 %copy-start.30 = (f32[1,2,1,2080]{3,2,1,0:T(1,128)S(1)}, f32[1,2,1,2080]{3,2,1,0:T(1,128)}, u32[]{:S(2)}) copy-start(f32[1,2,1,2080]{3,2,1,0:T(1,128)} %stack.494) | copy-start | bytes 49924
  188.3 10.6 %copy-start.31 = (f32[1,2,1,2080]{3,2,1,0:T(1,128)S(1)}, f32[1,2,1,2080]{3,2,1,0:T(1,128)}, u32[]{:S(2)}) copy-start(f32[1,2,1,2080]{3,2,1,0:T(1,128)} %stack.495) | copy-start | bytes 49924
  188.3 10.6 %copy-start.32 = (f32[1,2,1,2080]{3,2,1,0:T(1,128)S(1)}, f32[1,2,1,2080]{3,2,1,0:T(1,128)}, u32[]{:S(2)}) copy-start(f32[1,2,1,2080]{3,2,1,0:T(1,128)} %stack.496) | copy-start | bytes 49924
  188.3 10.6 %copy-start.33 = (f32[1,2,1,2080]{3,2,1,0:T(1,128)S(1)}, f32[1,2,1,2080]{3,2,1,0:T(1,128)}, u32[]{:S(2)}) copy-start(f32[1,2,1,2080]{3,2,1,0:T(1,128)} %stack.497) | copy-start | bytes 49924
  188.3 10.6 %copy-start.34 = (f32[1,2,1,2080]{3,2,1,0:T(1,128)S(1)}, f32[1,2,1,2080]{3,2,1,0:T(1,128)}, u32[]{:S(2)}) copy-start(f32[1,2,1,2080]{3,2,1,0:T(1,128)} %stack.498) | copy-start | bytes 49924
  188.4 10.6 %copy-start.35 = (f32[1,2,1,2080]{3,2,1,0:T(1,128)S(1)}, f32[1,2,1,2080]{3,2,1,0:T(1,128)}, u32[]{:S(2)}) copy-start(f32[1,2,1,2080]{3,2,1,0:T(1,128)} %stack.499) | copy-start | bytes 49924
  188.4 10.6 %copy-start.36 = (f32[1,2,1,2080]{3,2,1,0:T(1,128)S(1)}, f32[1,2,1,2080]{3,2,1,0:T(1,128)}, u32[]{:S(2)}) copy-start(f32[1,2,1,2080]{3,2,1,0:T(1,128)} %stack.500) | copy-start | bytes 49924
  194.6 10.0 %copy-start.41 = (f32[1,2,1,2080]{3,2,1,0:T(1,128)S(1)}, f32[1,2,1,2080]{3,2,1,0:T(1,128)}, u32[]{:S(2)}) copy-start(f32[1,2,1,2080]{3,2,1,0:T(1,128)} %stack.545) | copy-start | bytes 49924
  194.6 10.0 %copy-start.42 = (f32[1,2,1,2080]{3,2,1,0:T(1,128)S(1)}, f32[1,2,1,2080]{3,2,1,0:T(1,128)}, u32[]{:S(2)}) copy-start(f32[1,2,1,2080]{3,2,1,0:T(1,128)} %stack.546) | copy-start | bytes 49924
  194.6 10.0 %copy-start.43 = (f32[1,2,1,2080]{3,2,1,0:T(1,128)S(1)}, f32[1,2,1,2080]{3,2,1,0:T(1,128)}, u32[]{:S(2)}) copy-start(f32[1,2,1,2080]{3,2,1,0:T(1,128)} %stack.547) | copy-start | bytes 49924
  194.6 10.0 %copy-start.44 = (f32[1,2,1,2080]{3,2,1,0:T(1,128)S(1)}, f32[1,2,1,2080]{3,2,1,0:T(1,128)}, u32[]{:S(2)}) copy-start(f32[1,2,1,2080]{3,2,1,0:T(1,128)} %stack.548) | copy-start | bytes 49924
  194.6 10.0 %copy-start.45 = (f32[1,2,1,2080]{3,2,1,0:T(1,128)S(1)}, f32[1,2,1,2080]{3,2,1,0:T(1,128)}, u32[]{:S(2)}) copy-start(f32[1,2,1,2080]{3,2,1,0:T(1,128)} %stack.549) | copy-start | bytes 49924
  397.8 169.1 %copy-start.54 = (s32[16]{0:T(128)S(1)}, s32[16]{0:T(128)}, u32[]{:S(2)}) copy-start(s32[16]{0:T(128)} %copy-done.53) | copy-start | bytes 196
  555.1 20.7 %all-to-all-start.1 = ((f32[2,1,2,128]{0,2,1,3:T(2,128)}), f32[2,1,2,128]{0,2,1,3:T(2,128)S(1)}, u32[]{:S(2)}, u32[]{:S(2)}) async-start(f32[2,1,2,128]{0,2,1,3:T(2,128)} %copy.577), calls=%async_computation.1 | async-start | bytes 262144 | tf_op jit(solution)/shard_map/all_to_all | solution.py:132
  (14 other events, 99.3 us)
Sparse Core Ops, SparseCore 0:
  147.6 152.2 all-reduce.3
  303.1 79.4 all-gather.1
  402.2 151.3 all-reduce.5
where the time goes:
time: 587 us; the launch traced here: 583 us
  waiting for transfers between devices  313 us (53%)
  local copies, waits for them, and re-layouts  147 us (25%)
  blocking collectives  41.2 us (7%)
  other arithmetic  27.8 us (5%)
  starting transfers between devices  22.2 us (4%)
  matrix products  18.2 us (3%)
  between operations  14.9 us (3%)
    unnamed x4, waiting for transfers between devices  150 us
    psum x1, waiting for transfers between devices, body(): lax.psum(jnp.einsum('afbp,afbq->fpq', own_sketch, own_sketch, precision=h...  89 us
    all_gather x1, waiting for transfers between devices, body(): sketch = lax.all_gather(own_sketch, 'trace', axis=0, tiled=True)  58.3 us
    another operation x66, local copies, waits for them, and re-layouts, body(): jnp.stack([row_slabs[..., anchor:anchor + lag_y] for anchor in range(win_...  53 us
    another operation x68, local copies, waits for them, and re-layouts, body(): jnp.stack([band[:, :, anchor:anchor + win_x] for anchor in range(lag_x)],...  51 us
    all_gather x1, blocking collectives, body(): whole_slices = lax.all_gather(slices, 'trace', axis=2, tiled=True)  41.2 us
    slice x69, local copies, waits for them, and re-layouts, body(): row_slabs[..., anchor:anchor + lag_y]  21.6 us
    another operation x3, other arithmetic, body(): factor = jnp.linalg.cholesky(real_gram)  12.6 us
  transfers between devices with their start and end apart: 5, of which 5 were waited for; matrix products, arithmetic and copies ran while one was open for 15% of the time, Pallas kernels for 0%

commit v1 on v0

--- a/solution.py
+++ b/solution.py
@@ -6,6 +6,11 @@
 
 FREQ_DEV = 1
 highest = lax.Precision.HIGHEST
+
+
+def gather_by_exchange(x, axis, dim):
+    copies = jnp.concatenate([x] * lax.axis_size(axis), axis=dim)
+    return lax.all_to_all(copies, axis, dim, dim, tiled=True)
 
 
 def fourier_tables(samples, freq_total):
@@ -44,7 +49,7 @@
     spectrum = jnp.einsum("xyt,tpk->xypk", traces.astype(jnp.float32), forward, precision=highest)
     spectrum = lax.all_to_all(spectrum, "freq", split_axis=3, concat_axis=1, tiled=True)
     slices = jnp.transpose(spectrum, (3, 2, 0, 1))
-    whole_slices = lax.all_gather(slices, "trace", axis=2, tiled=True)
+    whole_slices = gather_by_exchange(slices, "trace", 2)
     freq_dev = whole_slices.shape[0]
     first_row = position * own_rows
     row_slabs = jnp.stack([lax.dynamic_slice_in_dim(whole_slices, first_row + 0, lag_x, 2)], axis=1)

time: 587 us -> 571 us (0.973)
  blocking collectives: 41.2 us -> 16.7 us
  local copies, waits for them, and re-layouts: 147 us -> 164 us
  waiting for transfers between devices: 313 us -> 301 us
    all_gather x1 -> x0, blocking collectives: 41.2 us -> none  [body(): whole_slices = lax.all_gather(slices, 'trace', axis=2, tiled=True)]
    unnamed x115 -> x146, local copies, waits for them, and re-layouts: 2.14 us -> 20.1 us
    all_to_all x0 -> x1, blocking collectives: none -> 16.7 us  [body(): lax.all_to_all(spectrum, 'freq', split_axis=3, concat_axis=1, tiled=True)]
    psum x1, waiting for transfers between devices: 89 us -> 76.2 us  [body(): lax.psum(jnp.einsum('afbp,afbq->fpq', own_sketch, own_sketch, precision=h...]
  transfers between devices with their start and end apart: 5 -> 5, of which waited for: 5 -> 5; matrix products, arithmetic and copies ran while one was open for 15% -> 16% of each run, Pallas kernels for 0% -> 0%
where the time goes in v1:
time: 571 us; the launch traced here: 567 us
  waiting for transfers between devices  301 us (53%)
  local copies, waits for them, and re-layouts  164 us (29%)
  other arithmetic  27.8 us (5%)
  starting transfers between devices  24 us (4%)
  matrix products  18.2 us (3%)
  blocking collectives  16.7 us (3%)
  between operations  14.9 us (3%)
    unnamed x4, waiting for transfers between devices  150 us
    psum x1, waiting for transfers between devices, body(): lax.psum(jnp.einsum('afbp,afbq->fpq', own_sketch, own_sketch, precision=h...  76.2 us
    all_gather x1, waiting for transfers between devices, body(): sketch = lax.all_gather(own_sketch, 'trace', axis=0, tiled=True)  58.3 us
    another operation x66, local copies, waits for them, and re-layouts, body(): jnp.stack([row_slabs[..., anchor:anchor + lag_y] for anchor in range(win_...  53 us
    another operation x68, local copies, waits for them, and re-layouts, body(): jnp.stack([band[:, :, anchor:anchor + win_x] for anchor in range(lag_x)],...  51 us
    slice x69, local copies, waits for them, and re-layouts, body(): row_slabs[..., anchor:anchor + lag_y]  21.6 us
    unnamed x146, local copies, waits for them, and re-layouts  20.1 us
    all_to_all x1, blocking collectives, body(): lax.all_to_all(spectrum, 'freq', split_axis=3, concat_axis=1, tiled=True)  16.7 us
  transfers between devices with their start and end apart: 5, of which 5 were waited for; matrix products, arithmetic and copies ran while one was open for 16% of the time, Pallas kernels for 0%

profile of v1, /device:TPU:1, one launch (start us, length us, event | category | flops | bytes accessed | tf_op | source)
XLA Modules:
  0.0 567.3 jit_solution(12122509520955512131)
XLA Ops:
  7.2 1.4 convolution_bitcast_fusion.5
  8.7 16.7 %all_to_all.41 = f32[2,8,2,16]{1,0,2,3:T(2,128)S(1)} all-to-all(f32[2,8,2,16]{1,0,2,3:T(2,128)S(1)} %copy.367), channel_id=1, replica_groups=mesh['freq'=16,'trace'=32] {'freq'}, dimensions={3} | all-to-all | bytes 4096 | tf_op jit(solution)/shard_map/all_to_all | solution.py:50
  44.0 12.0 %all-to-all-start.1 = ((f32[1,2,64,128]{3,1,0,2:T(2,128)}), f32[1,2,64,128]{3,1,0,2:T(2,128)S(1)}, u32[]{:S(2)}, u32[]{:S(2)}) async-start(f32[1,2,64,128]{3,1,0,2:T(2,128)} %bitcast.7), calls=%async_computation.1 | async-start | bytes 131072 | tf_op jit(solution)/shard_map/all_to_all | solution.py:13
  56.1 8.8 %all-to-all-done.1 = f32[1,2,64,128]{3,1,0,2:T(2,128)S(1)} async-done(((f32[1,2,64,128]{3,1,0,2:T(2,128)}), f32[1,2,64,128]{3,1,0,2:T(2,128)S(1)}, u32[]{:S(2)}, u32[]{:S(2)}) %all-to-all-start.1) | async-done | bytes 65568 | tf_op jit(solution)/shard_map/all_to_all | solution.py:13
  64.8 1.5 fusion.69
  66.4 1.4 fusion.68
  68.5 1.0 fusion.70
  69.6 0.8 copy.379
  71.0 0.8 copy.380
  72.4 0.8 copy.381
  73.9 0.8 copy.382
  75.3 0.8 copy.383
  76.8 0.8 copy.384
  78.2 0.8 copy.385
  79.7 0.8 copy.386
  81.1 0.8 copy.387
  82.6 0.8 copy.388
  84.0 0.8 copy.389
  85.5 0.8 copy.390
  86.9 0.8 copy.391
  88.4 0.8 copy.392
  89.8 0.8 copy.393
  91.3 0.8 copy.394
  92.8 0.8 copy.395
  98.5 0.8 copy.399
  100.0 0.8 copy.400
  130.5 9.0 %stack.490 = f32[2,65,2112]{2,1,0:T(8,128)S(1)} concatenate(f32[2,1,2112]{2,1,0:T(1,128)} %stack.562, f32[2,1,2112]{2,1,0:T(1,128)} %stack.563, f32[2,1,2112]{2,1,0:T(1,128)} %stack.564, f32[2,1,2112]{2,1,0:T(1,128)} %stack.565, f32[2,1,2112]{2,1,0:T(1,128)} %stack.566, f32[2,1,2112]{2,1,0:T(1,128)} %stack.567, f32[2,1,2112]{2,1,0:T(1,128)} %stack.568, f32[2,1,2112]{2,1,0:T(1,128)} %stack.569, ...), dimensions={1} | concatenate | bytes 2196480 | tf_op jit(solution)/shard_map/stack | solution.py:56
  139.5 3.6 fusion.6
  143.2 0.9 convolution_bitcast_fusion.3
  146.4 1.2 constant_dynamic-slice_fusion.65
  159.9 1.8 constant_dynamic-slice_fusion.47
  195.6 5.6 stack.524
  201.2 6.3 %stack.558 = f32[1,2,33,2080]{3,2,1,0:T(8,128)} concatenate(f32[1,2,1,2080]{3,2,1,0:T(1,128)S(1)} %copy-done.37, f32[1,2,1,2080]{3,2,1,0:T(1,128)} %stack.526, f32[1,2,1,2080]{3,2,1,0:T(1,128)} %stack.527, f32[1,2,1,2080]{3,2,1,0:T(1,128)} %stack.528, f32[1,2,1,2080]{3,2,1,0:T(1,128)S(1)} %copy-done.48, f32[1,2,1,2080]{3,2,1,0:T(1,128)S(1)} %copy-done.49, ...), dimensions={2} | concatenate | bytes 1098240 | tf_op jit(solution)/shard_map/stack | solution.py:73
  207.6 76.2 %all-reduce.4.cloned.1.call-done = f32[1,128,128]{1,2,0:T(8,128)} async-done(((f32[1,128,128]{1,2,0:T(8,128)}), f32[1,128,128]{1,2,0:T(8,128)}) %all-reduce.4.cloned.1.call-update) | async-done | bytes 65552 | tf_op jit(solution)/shard_map/psum | solution.py:65
  283.8 0.9 fusion.66
  285.0 11.9 %custom-call.11 = f32[1,128,128]{2,1,0:T(8,128)S(1)} custom-call(f32[1,128,128]{2,1,0:T(8,128)S(1)} %fusion.46), custom_call_target="Cholesky" | custom-call | tf_op jit(solution)/shard_map/jit(cholesky)/cholesky | solution.py:98
  298.3 9.8 %custom-call.12 = f32[1,1,128,128]{2,3,1,0:T(8,128)S(1)} custom-call(f32[1,1,128,128]{3,2,1,0:T(8,128)S(1)} %fusion.41), custom_call_target="InvertDiagBlocksLowerTriangular" | custom-call | tf_op jit(solution)/shard_map/vmap(jit(_cho_solve))/triangular_solve | solution.py:30
  308.1 58.3 %all-gather.2.cloned.1.call-done = f32[32,1,65,128]{3,1,2,0:T(1,128)} async-done(((f32[1,1,65,128]{3,1,2,0:T(1,128)}), f32[32,1,65,128]{3,1,2,0:T(1,128)}) %all-gather.2.cloned.1.call-update) | async-done | bytes 1064976 | tf_op jit(solution)/shard_map/all_gather | solution.py:64
  366.4 3.1 fusion.9
  370.5 5.1 convolution_bitcast_fusion.1
  375.6 6.0 %copy.575 = f32[1,65,2,2,33,32]{1,5,4,3,2,0:T(8,128)} copy(f32[1,65,2,2,33,32]{4,5,3,2,1,0:T(8,128)} %convolution_bitcast_fusion.1) | data formatting | bytes 2196480 | tf_op jit(solution)/shard_map/fqezc,fbqa->fbezca/transpose | solution.py:110
  381.6 2.6 convolution_bitcast_fusion.2
  386.0 1.3 dynamic-slice.1
  388.0 149.5 %all-reduce.6.cloned.1.call-done = f32[64,1,2,128]{3,0,2,1:T(8,128)} async-done(((f32[64,1,2,128]{3,0,2,1:T(8,128)}), f32[64,1,2,128]{3,0,2,1:T(8,128)}) %all-reduce.6.cloned.1.call-update) | async-done | bytes 65552
  538.1 0.8 copy.577
  538.9 11.8 %all-to-all-start.2 = ((f32[2,1,2,128]{0,2,1,3:T(2,128)}), f32[2,1,2,128]{0,2,1,3:T(2,128)S(1)}, u32[]{:S(2)}, u32[]{:S(2)}) async-start(f32[2,1,2,128]{0,2,1,3:T(2,128)} %copy.577), calls=%async_computation.2 | async-start | bytes 262144 | tf_op jit(solution)/shard_map/all_to_all | solution.py:137
  551.3 8.3 %all-to-all-done.2 = f32[2,1,2,128]{0,2,1,3:T(2,128)S(1)} async-done(((f32[2,1,2,128]{0,2,1,3:T(2,128)}), f32[2,1,2,128]{0,2,1,3:T(2,128)S(1)}, u32[]{:S(2)}, u32[]{:S(2)}) %all-to-all-start.2) | async-done | bytes 2080 | tf_op jit(solution)/shard_map/all_to_all | solution.py:137
  559.8 1.0 convolution_bitcast_fusion
  (434 shorter events, 120.1 us)
Async XLA Ops:
  6.5 133.0 %copy-start = (f32[2,33,64,64]{3,2,1,0:T(8,128)S(1)}, f32[2,33,64,64]{3,2,1,0:T(8,128)}, u32[]{:S(2)}) copy-start(f32[2,33,64,64]{3,2,1,0:T(8,128)} %param.3) | copy-start | bytes 3244036
  44.0 20.8 %all-to-all-start.1 = ((f32[1,2,64,128]{3,1,0,2:T(2,128)}), f32[1,2,64,128]{3,1,0,2:T(2,128)S(1)}, u32[]{:S(2)}, u32[]{:S(2)}) async-start(f32[1,2,64,128]{3,1,0,2:T(2,128)} %bitcast.7), calls=%async_computation.1 | async-start | bytes 131072 | tf_op jit(solution)/shard_map/all_to_all | solution.py:13
  56.0 227.8 %all-reduce.4.cloned.1.call-start = ((), (), s32[]{:S(2)}) async-start(), calls=%async_computation.4 | async-start | bytes 131072 | tf_op jit(solution)/shard_map/psum | solution.py:65
  110.4 14.5 %copy-start.10 = (f32[1,1,2,33,64]{4,2,3,1,0:T(2,128)S(1)}, f32[1,1,2,33,64]{4,2,3,1,0:T(2,128)}, u32[]{:S(2)}) copy-start(f32[1,1,2,33,64]{4,2,3,1,0:T(2,128)} %get-tuple-element.145) | copy-start | bytes 50692
  111.1 14.5 %copy-start.9 = (f32[1,1,2,33,64]{4,2,3,1,0:T(2,128)S(1)}, f32[1,1,2,33,64]{4,2,3,1,0:T(2,128)}, u32[]{:S(2)}) copy-start(f32[1,1,2,33,64]{4,2,3,1,0:T(2,128)} %get-tuple-element.144) | copy-start | bytes 50692
  111.8 14.6 %copy-start.8 = (f32[1,1,2,33,64]{4,2,3,1,0:T(2,128)S(1)}, f32[1,1,2,33,64]{4,2,3,1,0:T(2,128)}, u32[]{:S(2)}) copy-start(f32[1,1,2,33,64]{4,2,3,1,0:T(2,128)} %get-tuple-element.143) | copy-start | bytes 50692
  112.5 14.5 %copy-start.7 = (f32[1,1,2,33,64]{4,2,3,1,0:T(2,128)S(1)}, f32[1,1,2,33,64]{4,2,3,1,0:T(2,128)}, u32[]{:S(2)}) copy-start(f32[1,1,2,33,64]{4,2,3,1,0:T(2,128)} %get-tuple-element.142) | copy-start | bytes 50692
  113.2 14.5 %copy-start.6 = (f32[1,1,2,33,64]{4,2,3,1,0:T(2,128)S(1)}, f32[1,1,2,33,64]{4,2,3,1,0:T(2,128)}, u32[]{:S(2)}) copy-start(f32[1,1,2,33,64]{4,2,3,1,0:T(2,128)} %get-tuple-element.141) | copy-start | bytes 50692
  113.9 14.5 %copy-start.5 = (f32[1,1,2,33,64]{4,2,3,1,0:T(2,128)S(1)}, f32[1,1,2,33,64]{4,2,3,1,0:T(2,128)}, u32[]{:S(2)}) copy-start(f32[1,1,2,33,64]{4,2,3,1,0:T(2,128)} %get-tuple-element.140) | copy-start | bytes 50692
  114.6 14.6 %copy-start.4 = (f32[1,1,2,33,64]{4,2,3,1,0:T(2,128)S(1)}, f32[1,1,2,33,64]{4,2,3,1,0:T(2,128)}, u32[]{:S(2)}) copy-start(f32[1,1,2,33,64]{4,2,3,1,0:T(2,128)} %get-tuple-element.139) | copy-start | bytes 50692
  115.3 14.5 %copy-start.3 = (f32[1,1,2,33,64]{4,2,3,1,0:T(2,128)S(1)}, f32[1,1,2,33,64]{4,2,3,1,0:T(2,128)}, u32[]{:S(2)}) copy-start(f32[1,1,2,33,64]{4,2,3,1,0:T(2,128)} %get-tuple-element.138) | copy-start | bytes 50692
  116.0 14.6 %copy-start.51 = (f32[2,1,2112]{2,1,0:T(1,128)S(1)}, f32[2,1,2112]{2,1,0:T(1,128)}, u32[]{:S(2)}) copy-start(f32[2,1,2112]{2,1,0:T(1,128)} %stack.571) | copy-start | bytes 50692
  116.0 14.6 %copy-start.52 = (f32[2,1,2112]{2,1,0:T(1,128)S(1)}, f32[2,1,2112]{2,1,0:T(1,128)}, u32[]{:S(2)}) copy-start(f32[2,1,2112]{2,1,0:T(1,128)} %stack.572) | copy-start | bytes 50692
  144.1 222.4 %all-gather.2.cloned.1.call-start = ((), (), s32[]{:S(2)}) async-start(), calls=%async_computation.3 | async-start | bytes 1098240 | tf_op jit(solution)/shard_map/all_gather | solution.py:64
  144.9 392.5 %all-reduce.6.cloned.1.call-start = ((), (), s32[]{:S(2)}) async-start(), calls=%async_computation.5 | async-start | bytes 131072
  184.7 10.6 %copy-start.11 = (f32[1,2,1,2080]{3,2,1,0:T(1,128)S(1)}, f32[1,2,1,2080]{3,2,1,0:T(1,128)}, u32[]{:S(2)}) copy-start(f32[1,2,1,2080]{3,2,1,0:T(1,128)} %stack.491) | copy-start | bytes 49924
  184.7 10.6 %copy-start.12 = (f32[1,2,1,2080]{3,2,1,0:T(1,128)S(1)}, f32[1,2,1,2080]{3,2,1,0:T(1,128)}, u32[]{:S(2)}) copy-start(f32[1,2,1,2080]{3,2,1,0:T(1,128)} %stack.508) | copy-start | bytes 49924
  184.7 10.6 %copy-start.13 = (f32[1,2,1,2080]{3,2,1,0:T(1,128)S(1)}, f32[1,2,1,2080]{3,2,1,0:T(1,128)}, u32[]{:S(2)}) copy-start(f32[1,2,1,2080]{3,2,1,0:T(1,128)} %stack.509) | copy-start | bytes 49924
  184.7 10.6 %copy-start.14 = (f32[1,2,1,2080]{3,2,1,0:T(1,128)S(1)}, f32[1,2,1,2080]{3,2,1,0:T(1,128)}, u32[]{:S(2)}) copy-start(f32[1,2,1,2080]{3,2,1,0:T(1,128)} %stack.510) | copy-start | bytes 49924
  184.7 10.6 %copy-start.15 = (f32[1,2,1,2080]{3,2,1,0:T(1,128)S(1)}, f32[1,2,1,2080]{3,2,1,0:T(1,128)}, u32[]{:S(2)}) copy-start(f32[1,2,1,2080]{3,2,1,0:T(1,128)} %stack.511) | copy-start | bytes 49924
  184.8 10.6 %copy-start.16 = (f32[1,2,1,2080]{3,2,1,0:T(1,128)S(1)}, f32[1,2,1,2080]{3,2,1,0:T(1,128)}, u32[]{:S(2)}) copy-start(f32[1,2,1,2080]{3,2,1,0:T(1,128)} %stack.512) | copy-start | bytes 49924
  184.8 10.6 %copy-start.17 = (f32[1,2,1,2080]{3,2,1,0:T(1,128)S(1)}, f32[1,2,1,2080]{3,2,1,0:T(1,128)}, u32[]{:S(2)}) copy-start(f32[1,2,1,2080]{3,2,1,0:T(1,128)} %stack.513) | copy-start | bytes 49924
  184.8 10.6 %copy-start.18 = (f32[1,2,1,2080]{3,2,1,0:T(1,128)S(1)}, f32[1,2,1,2080]{3,2,1,0:T(1,128)}, u32[]{:S(2)}) copy-start(f32[1,2,1,2080]{3,2,1,0:T(1,128)} %stack.514) | copy-start | bytes 49924
  184.8 10.6 %copy-start.19 = (f32[1,2,1,2080]{3,2,1,0:T(1,128)S(1)}, f32[1,2,1,2080]{3,2,1,0:T(1,128)}, u32[]{:S(2)}) copy-start(f32[1,2,1,2080]{3,2,1,0:T(1,128)} %stack.515) | copy-start | bytes 49924
  184.8 10.6 %copy-start.20 = (f32[1,2,1,2080]{3,2,1,0:T(1,128)S(1)}, f32[1,2,1,2080]{3,2,1,0:T(1,128)}, u32[]{:S(2)}) copy-start(f32[1,2,1,2080]{3,2,1,0:T(1,128)} %stack.516) | copy-start | bytes 49924
  184.8 10.6 %copy-start.21 = (f32[1,2,1,2080]{3,2,1,0:T(1,128)S(1)}, f32[1,2,1,2080]{3,2,1,0:T(1,128)}, u32[]{:S(2)}) copy-start(f32[1,2,1,2080]{3,2,1,0:T(1,128)} %stack.517) | copy-start | bytes 49924
  184.8 10.6 %copy-start.22 = (f32[1,2,1,2080]{3,2,1,0:T(1,128)S(1)}, f32[1,2,1,2080]{3,2,1,0:T(1,128)}, u32[]{:S(2)}) copy-start(f32[1,2,1,2080]{3,2,1,0:T(1,128)} %stack.518) | copy-start | bytes 49924
  184.8 10.6 %copy-start.23 = (f32[1,2,1,2080]{3,2,1,0:T(1,128)S(1)}, f32[1,2,1,2080]{3,2,1,0:T(1,128)}, u32[]{:S(2)}) copy-start(f32[1,2,1,2080]{3,2,1,0:T(1,128)} %stack.519) | copy-start | bytes 49924
  184.8 10.6 %copy-start.24 = (f32[1,2,1,2080]{3,2,1,0:T(1,128)S(1)}, f32[1,2,1,2080]{3,2,1,0:T(1,128)}, u32[]{:S(2)}) copy-start(f32[1,2,1,2080]{3,2,1,0:T(1,128)} %stack.520) | copy-start | bytes 49924
  184.8 10.6 %copy-start.25 = (f32[1,2,1,2080]{3,2,1,0:T(1,128)S(1)}, f32[1,2,1,2080]{3,2,1,0:T(1,128)}, u32[]{:S(2)}) copy-start(f32[1,2,1,2080]{3,2,1,0:T(1,128)} %stack.521) | copy-start | bytes 49924
  184.9 10.6 %copy-start.26 = (f32[1,2,1,2080]{3,2,1,0:T(1,128)S(1)}, f32[1,2,1,2080]{3,2,1,0:T(1,128)}, u32[]{:S(2)}) copy-start(f32[1,2,1,2080]{3,2,1,0:T(1,128)} %stack.522) | copy-start | bytes 49924
  184.9 10.6 %copy-start.27 = (f32[1,2,1,2080]{3,2,1,0:T(1,128)S(1)}, f32[1,2,1,2080]{3,2,1,0:T(1,128)}, u32[]{:S(2)}) copy-start(f32[1,2,1,2080]{3,2,1,0:T(1,128)} %stack.523) | copy-start | bytes 49924
  184.9 10.6 %copy-start.28 = (f32[1,2,1,2080]{3,2,1,0:T(1,128)S(1)}, f32[1,2,1,2080]{3,2,1,0:T(1,128)}, u32[]{:S(2)}) copy-start(f32[1,2,1,2080]{3,2,1,0:T(1,128)} %stack.492) | copy-start | bytes 49924
  184.9 10.6 %copy-start.29 = (f32[1,2,1,2080]{3,2,1,0:T(1,128)S(1)}, f32[1,2,1,2080]{3,2,1,0:T(1,128)}, u32[]{:S(2)}) copy-start(f32[1,2,1,2080]{3,2,1,0:T(1,128)} %stack.493) | copy-start | bytes 49924
  184.9 10.6 %copy-start.30 = (f32[1,2,1,2080]{3,2,1,0:T(1,128)S(1)}, f32[1,2,1,2080]{3,2,1,0:T(1,128)}, u32[]{:S(2)}) copy-start(f32[1,2,1,2080]{3,2,1,0:T(1,128)} %stack.494) | copy-start | bytes 49924
  184.9 10.6 %copy-start.31 = (f32[1,2,1,2080]{3,2,1,0:T(1,128)S(1)}, f32[1,2,1,2080]{3,2,1,0:T(1,128)}, u32[]{:S(2)}) copy-start(f32[1,2,1,2080]{3,2,1,0:T(1,128)} %stack.495) | copy-start | bytes 49924
  184.9 10.6 %copy-start.32 = (f32[1,2,1,2080]{3,2,1,0:T(1,128)S(1)}, f32[1,2,1,2080]{3,2,1,0:T(1,128)}, u32[]{:S(2)}) copy-start(f32[1,2,1,2080]{3,2,1,0:T(1,128)} %stack.496) | copy-start | bytes 49924
  184.9 10.6 %copy-start.33 = (f32[1,2,1,2080]{3,2,1,0:T(1,128)S(1)}, f32[1,2,1,2080]{3,2,1,0:T(1,128)}, u32[]{:S(2)}) copy-start(f32[1,2,1,2080]{3,2,1,0:T(1,128)} %stack.497) | copy-start | bytes 49924
  184.9 10.6 %copy-start.34 = (f32[1,2,1,2080]{3,2,1,0:T(1,128)S(1)}, f32[1,2,1,2080]{3,2,1,0:T(1,128)}, u32[]{:S(2)}) copy-start(f32[1,2,1,2080]{3,2,1,0:T(1,128)} %stack.498) | copy-start | bytes 49924
  184.9 10.6 %copy-start.35 = (f32[1,2,1,2080]{3,2,1,0:T(1,128)S(1)}, f32[1,2,1,2080]{3,2,1,0:T(1,128)}, u32[]{:S(2)}) copy-start(f32[1,2,1,2080]{3,2,1,0:T(1,128)} %stack.499) | copy-start | bytes 49924
  185.0 10.6 %copy-start.36 = (f32[1,2,1,2080]{3,2,1,0:T(1,128)S(1)}, f32[1,2,1,2080]{3,2,1,0:T(1,128)}, u32[]{:S(2)}) copy-start(f32[1,2,1,2080]{3,2,1,0:T(1,128)} %stack.500) | copy-start | bytes 49924
  191.2 10.0 %copy-start.41 = (f32[1,2,1,2080]{3,2,1,0:T(1,128)S(1)}, f32[1,2,1,2080]{3,2,1,0:T(1,128)}, u32[]{:S(2)}) copy-start(f32[1,2,1,2080]{3,2,1,0:T(1,128)} %stack.545) | copy-start | bytes 49924
  191.2 10.0 %copy-start.42 = (f32[1,2,1,2080]{3,2,1,0:T(1,128)S(1)}, f32[1,2,1,2080]{3,2,1,0:T(1,128)}, u32[]{:S(2)}) copy-start(f32[1,2,1,2080]{3,2,1,0:T(1,128)} %stack.546) | copy-start | bytes 49924
  191.2 10.0 %copy-start.43 = (f32[1,2,1,2080]{3,2,1,0:T(1,128)S(1)}, f32[1,2,1,2080]{3,2,1,0:T(1,128)}, u32[]{:S(2)}) copy-start(f32[1,2,1,2080]{3,2,1,0:T(1,128)} %stack.547) | copy-start | bytes 49924
  191.2 10.0 %copy-start.44 = (f32[1,2,1,2080]{3,2,1,0:T(1,128)S(1)}, f32[1,2,1,2080]{3,2,1,0:T(1,128)}, u32[]{:S(2)}) copy-start(f32[1,2,1,2080]{3,2,1,0:T(1,128)} %stack.548) | copy-start | bytes 49924
  191.2 10.0 %copy-start.45 = (f32[1,2,1,2080]{3,2,1,0:T(1,128)S(1)}, f32[1,2,1,2080]{3,2,1,0:T(1,128)}, u32[]{:S(2)}) copy-start(f32[1,2,1,2080]{3,2,1,0:T(1,128)} %stack.549) | copy-start | bytes 49924
  381.6 169.1 %copy-start.54 = (s32[16]{0:T(128)S(1)}, s32[16]{0:T(128)}, u32[]{:S(2)}) copy-start(s32[16]{0:T(128)} %copy-done.53) | copy-start | bytes 196
  538.9 20.7 %all-to-all-start.2 = ((f32[2,1,2,128]{0,2,1,3:T(2,128)}), f32[2,1,2,128]{0,2,1,3:T(2,128)S(1)}, u32[]{:S(2)}, u32[]{:S(2)}) async-start(f32[2,1,2,128]{0,2,1,3:T(2,128)} %copy.577), calls=%async_computation.2 | async-start | bytes 262144 | tf_op jit(solution)/shard_map/all_to_all | solution.py:137
  (14 other events, 99.3 us)
Sparse Core Ops, SparseCore 0:
  144.2 139.5 all-reduce.3
  287.0 79.4 all-gather.1
  386.1 151.3 all-reduce.5
